TPU v7x, 512 devices: a whole 4x4x16 slice. The times are simulated.
512 devices in a mesh: band: 8 (over x_lo, y), xy: 64 (over z, x_hi, core).
Axes of the slice: x: 4 (x_hi: 2, x_lo: 2; x = x_hi * 2 + x_lo), y: 4, z: 16, core: 2. Of those that a mesh axis runs over, the one named last changes fastest.
Arguments:
- orbitals: float32 [16, 64, 128, 256], P('band', 'xy'), may hold values from -6 to 6
- energies: float32 [16], P('band'), may hold values from -1.5 to -0.25
- occupation: int32 [16], P('band'), may hold values from 1 to 2
- potential: float32 [64, 128, 256], P('xy'), may hold values from 0.25 to 2
- trials: float32 [4, 64, 128, 256], P(None, 'xy'), may hold values from -8 to 23
Outputs:
- density: float32 [4, 64, 128, 256], P(None, 'xy', 'band')
- response_matrix: float32 [4, 4], replicated
All inputs are finite; a program needn't handle non-finite values.
Results may differ from a plain program's by a relative error of at most 0.0001.
Values sent between devices are 32-bit elements; how exact they have to be, the bound alone decides.
No kernel may reach another device: no remote copies, remote signals or barrier semaphores. Data moves between devices by JAX's collectives and lax.ppermute only.
A program may use at most 64 MiB of HBM per device.

v0:
```python
import math
import jax
import jax.numpy as jnp
from jax import lax
from jax.sharding import PartitionSpec as P

ITERS = 3


def padded_2(block, sides, width):
    for axis, dim in sides:
        count = lax.axis_size(axis)
        forward = [(i, i + 1) for i in range(count - 1)]
        forward.append((count - 1, 0))
        backward = [(target, source) for source, target in forward]
        low = lax.ppermute(
            lax.slice_in_dim(block, block.shape[dim] - width, None, axis=dim), axis, forward
        )
        high = lax.ppermute(lax.slice_in_dim(block, 0, width, axis=dim), axis, backward)
        block = jnp.concatenate([low, block, high], axis=dim)
    return block


def respond(psi_rows, energy_rows, weight_rows, potential_part, trial_part, project, apply_op):
    orbital_count, cell_count = psi_rows.shape
    trial_count = trial_part.shape[0]
    row_count = orbital_count * trial_count
    diagonal_op = 3.0 + potential_part.reshape(1, 1, cell_count) - energy_rows[:, None, None]
    diagonal_op = jnp.broadcast_to(diagonal_op, (orbital_count, trial_count, cell_count)).reshape(
        row_count, cell_count
    )
    products = trial_part[None, :, :] * psi_rows[:, None, :]
    right_side = -project(products.reshape(row_count, cell_count))
    update = project(right_side / diagonal_op)
    for iteration in range(ITERS):
        residual = right_side - apply_op(update, diagonal_op)
        update = update + project(residual / diagonal_op)
    weights = weight_rows[:, None, None] * psi_rows[:, None, :]
    return jnp.sum(weights * update.reshape(orbital_count, trial_count, cell_count), axis=0)


def neighbours_z(field_block):
    z_padded = jnp.pad(field_block, ((0, 0), (0, 0), (0, 0), (1, 1)))
    return z_padded[..., 2:] + z_padded[..., :-2]


def local(orbitals, energies, occupation, potential, trials):
    nb_dev, width_x, width_y, width_z = orbitals.shape
    trial_count = trials.shape[0]
    cell_count = width_x * width_y * width_z
    cell_total = cell_count * lax.axis_size("xy")
    orbital_total = nb_dev * lax.axis_size("band")
    y_share = width_y // lax.axis_size("band")
    band_index = lax.axis_index("band")
    highest = lax.Precision.HIGHEST
    trial_slice = lax.dynamic_slice_in_dim(trials, band_index * y_share, y_share, 2)
    psi_flat = orbitals.reshape(nb_dev, cell_count)
    psi_all = lax.all_gather(psi_flat, "band", axis=0, tiled=True)

    def project_slab(vectors):
        intersection = jnp.dot(
            psi_all, vectors.T, precision=highest, preferred_element_type=jnp.float32
        )
        intersection = lax.psum(intersection, "xy") / cell_total
        return vectors - jnp.dot(
            intersection.T, psi_all, precision=highest, preferred_element_type=jnp.float32
        )

    def apply_slab(vectors, diagonal_op):
        field_block = vectors.reshape(-1, width_x, width_y, width_z)
        padded = padded_2(field_block, (("xy", 1),), 1)
        beside = padded[:, 2:] + padded[:, :-2]
        beside = beside + jnp.roll(field_block, 1, 2) + jnp.roll(field_block, -1, 2)
        beside = beside + neighbours_z(field_block)
        return diagonal_op * vectors - 0.5 * beside.reshape(vectors.shape)

    summed = respond(
        psi_flat,
        energies,
        occupation.astype(jnp.float32),
        potential.reshape(cell_count),
        trials.reshape(trial_count, cell_count),
        project_slab,
        apply_slab,
    )
    partial_grid = (summed / math.sqrt(orbital_total)).reshape(
        trial_count, width_x, width_y, width_z
    )
    density = lax.psum_scatter(partial_grid, "band", scatter_dimension=2, tiled=True)
    local_sum = jnp.dot(
        density.reshape(trial_count, -1),
        trial_slice.reshape(trial_count, -1).T,
        precision=highest,
        preferred_element_type=jnp.float32,
    )
    response_matrix = lax.psum(local_sum, ("band", "xy")) / cell_total
    return (density, response_matrix)


def solution(mesh):
    in_specs = (
        P("band", "xy", None, None),
        P("band"),
        P("band"),
        P("xy", None, None),
        P(None, "xy", None, None),
    )
    out_specs = (P(None, "xy", "band", None), P())
    return jax.shard_map(local, mesh=mesh, in_specs=in_specs, out_specs=out_specs, check_vma=False)
```

profile of v0, /device:TPU:1, one launch (start us, length us, event | category | flops | bytes accessed | tf_op | source)
XLA Modules:
  0.0 987.3 jit_solution(15164408557984125261)
XLA Ops:
  7.2 1.8 reshape.121
  12.4 1.4 mul.77
  13.7 45.2 %all-gather.3.cloned.1.call-done = f32[8,2,32768]{2,1,0:T(2,128)} async-done(((f32[1,2,32768]{2,1,0:T(2,128)}), f32[8,2,32768]{2,1,0:T(2,128)}) %all-gather.3.cloned.1.call-update) | async-done | bytes 2097168 | tf_op jit(solution)/shard_map/all_gather | solution.py:58
  58.9 2.7 reshape.122
  61.6 3.8 convolution_bitcast_fusion.4
  65.4 135.0 %psum.42 = f32[16,8]{0,1:T(8,128)S(1)} all-reduce(f32[16,8]{0,1:T(8,128)S(1)} %convolution_bitcast_fusion.4), channel_id=1, replica_groups=mesh['band'=8,'xy'=64] {'xy'}, use_global_device_ids=true, to_apply=%region_0.0 | all-reduce | flops 128 | bytes 1024 | tf_op jit(solution)/shard_map/psum | solution.py:64
  200.4 3.4 fusion.40
  204.8 2.5 convolution_bitcast_fusion.3
  207.4 128.3 %psum.43 = f32[16,8]{0,1:T(8,128)S(1)} all-reduce(f32[16,8]{0,1:T(8,128)S(1)} %convolution_bitcast_fusion.3), channel_id=1, replica_groups=mesh['band'=8,'xy'=64] {'xy'}, use_global_device_ids=true, to_apply=%region_1.0 | all-reduce | flops 128 | bytes 1024 | tf_op jit(solution)/shard_map/psum | solution.py:64
  335.7 2.3 convolution_subtract_fusion.3
  338.0 2.9 collective-permute-start
  340.9 4.4 collective-permute-start.1
  345.4 21.4 %collective-permute-done = f32[8,1,128,256]{3,0,2,1:T(8,128)S(1)} collective-permute-done((f32[8,1,128,256]{3,0,2,1:T(8,128)S(1)}, f32[8,1,128,256]{3,0,2,1:T(8,128)S(1)}, u32[]{:S(2)}, u32[]{:S(2)}) %collective-permute-start) | collective-permute-done | bytes 1048608 | tf_op jit(solution)/shard_map/ppermute | solution.py:19
  368.5 2.7 convolution_bitcast_fusion.2
  371.2 124.7 %psum.44 = f32[16,8]{0,1:T(8,128)S(1)} all-reduce(f32[16,8]{0,1:T(8,128)S(1)} %convolution_bitcast_fusion.2), channel_id=1, replica_groups=mesh['band'=8,'xy'=64] {'xy'}, use_global_device_ids=true, to_apply=%region_2.3 | all-reduce | flops 128 | bytes 1024 | tf_op jit(solution)/shard_map/psum | solution.py:64
  495.9 3.1 fusion.2
  499.1 6.5 collective-permute-start.2
  505.5 1.9 collective-permute-start.3
  507.7 20.3 %collective-permute-done.2 = f32[8,1,128,256]{3,0,2,1:T(8,128)S(1)} collective-permute-done((f32[8,1,128,256]{3,0,2,1:T(8,128)S(1)}, f32[8,1,128,256]{3,0,2,1:T(8,128)S(1)}, u32[]{:S(2)}, u32[]{:S(2)}) %collective-permute-start.2) | collective-permute-done | bytes 1048608 | tf_op jit(solution)/shard_map/ppermute | solution.py:19
  529.6 2.7 convolution_bitcast_fusion.1
  532.3 127.0 %psum.45 = f32[16,8]{0,1:T(8,128)S(1)} all-reduce(f32[16,8]{0,1:T(8,128)S(1)} %convolution_bitcast_fusion.1), channel_id=1, replica_groups=mesh['band'=8,'xy'=64] {'xy'}, use_global_device_ids=true, to_apply=%region_3.4 | all-reduce | flops 128 | bytes 1024 | tf_op jit(solution)/shard_map/psum | solution.py:64
  659.3 3.1 fusion.1
  662.4 4.2 collective-permute-start.4
  666.6 2.9 collective-permute-start.5
  670.5 20.8 %collective-permute-done.4 = f32[8,1,128,256]{3,0,2,1:T(8,128)S(1)} collective-permute-done((f32[8,1,128,256]{3,0,2,1:T(8,128)S(1)}, f32[8,1,128,256]{3,0,2,1:T(8,128)S(1)}, u32[]{:S(2)}, u32[]{:S(2)}) %collective-permute-start.4) | collective-permute-done | bytes 1048608 | tf_op jit(solution)/shard_map/ppermute | solution.py:19
  692.9 2.7 convolution_bitcast_fusion
  695.6 124.9 %psum.46 = f32[16,8]{0,1:T(8,128)S(1)} all-reduce(f32[16,8]{0,1:T(8,128)S(1)} %convolution_bitcast_fusion), channel_id=1, replica_groups=mesh['band'=8,'xy'=64] {'xy'}, use_global_device_ids=true, to_apply=%region_4.5 | all-reduce | flops 128 | bytes 1024 | tf_op jit(solution)/shard_map/psum | solution.py:64
  820.5 4.1 fusion
  824.7 1.6 reshape.118
  828.6 41.6 %reduce-scatter.2.cloned.1.call-done = f32[4,1,16,256]{3,2,1,0:T(8,128)} async-done(((f32[4,1,128,256]{3,2,1,0:T(8,128)}), f32[4,1,16,256]{3,2,1,0:T(8,128)}) %reduce-scatter.2.cloned.1.call-update) | async-done | bytes 65552 | tf_op jit(solution)/shard_map/reduce_scatter | solution.py:89
  870.1 1.2 convolution_bitcast_fusion.5
  871.4 108.6 %psum.47 = f32[4,4]{1,0:T(4,128)S(1)} all-reduce(f32[4,4]{1,0:T(4,128)S(1)} %convolution_bitcast_fusion.5), channel_id=1, replica_groups=mesh['band'=8,'xy'=64] {'band','xy'}, use_global_device_ids=true, to_apply=%region_7.8 | all-reduce | flops 16 | bytes 128 | tf_op jit(solution)/shard_map/psum | solution.py:96
  (59 shorter events, 13.3 us)
Async XLA Ops:
  7.2 51.8 %all-gather.3.cloned.1.call-start = ((), (), s32[]{:S(2)}) async-start(), calls=%async_computation.2 | async-start | bytes 2359296 | tf_op jit(solution)/shard_map/all_gather | solution.py:58
  9.1 861.1 %reduce-scatter.2.cloned.1.call-start = ((), (), s32[]{:S(2)}) async-start(), calls=%async_computation.1 | async-start | bytes 589824 | tf_op jit(solution)/shard_map/reduce_scatter | solution.py:89
  10.0 1.5 copy-start.11
  10.1 1.7 copy-start.12
  203.9 1.0 copy-start.6
  338.0 29.5 %copy-start.5 = (f32[8,32768]{1,0:T(8,128)}, f32[8,32768]{1,0:T(8,128)S(1)}, u32[]{:S(2)}) copy-start(f32[8,32768]{1,0:T(8,128)S(1)} %convolution_subtract_fusion.3) | copy-start | bytes 3145732
  338.0 28.9 %collective-permute-start = (f32[8,1,128,256]{3,0,2,1:T(8,128)S(1)}, f32[8,1,128,256]{3,0,2,1:T(8,128)S(1)}, u32[]{:S(2)}, u32[]{:S(2)}) collective-permute-start(f32[8,1,128,256]{3,0,2,1:T(8,128)S(1)} %bitcast.60), channel_id=1, source_target_pairs={{1,0},{2,1},{3,2},{4,3},{5,4},{6,5},{7,6},{8,7},{9,8},{10,9},{11,1... | collective-permute-start | bytes 3145736 | tf_op jit(solution)/shard_map/ppermute | solution.py:19
  340.9 26.0 %collective-permute-start.1 = (f32[8,1,128,256]{3,0,2,1:T(8,128)S(1)}, f32[8,1,128,256]{3,0,2,1:T(8,128)S(1)}, u32[]{:S(2)}, u32[]{:S(2)}) collective-permute-start(f32[8,1,128,256]{3,0,2,1:T(8,128)S(1)} %bitcast.61), channel_id=1, source_target_pairs={{0,1},{1,2},{2,3},{3,4},{4,5},{5,6},{6,7},{7,8},{8,9},{9,10},{10,1... | collective-permute-start | bytes 3145736 | tf_op jit(solution)/shard_map/ppermute | solution.py:16
  366.9 1.7 copy-start
  367.5 1.0 copy-start.8
  495.9 11.6 %copy-start.13 = (s32[2]{0:T(128)S(1)}, s32[2]{0:T(128)}, u32[]{:S(2)}) copy-start(s32[2]{0:T(128)} %param.7) | copy-start | bytes 28
  499.1 29.5 %copy-start.4 = (f32[8,32768]{1,0:T(8,128)}, f32[8,32768]{1,0:T(8,128)S(1)}, u32[]{:S(2)}) copy-start(f32[8,32768]{1,0:T(8,128)S(1)} %fusion.2) | copy-start | bytes 3145732
  499.1 28.9 %collective-permute-start.2 = (f32[8,1,128,256]{3,0,2,1:T(8,128)S(1)}, f32[8,1,128,256]{3,0,2,1:T(8,128)S(1)}, u32[]{:S(2)}, u32[]{:S(2)}) collective-permute-start(f32[8,1,128,256]{3,0,2,1:T(8,128)S(1)} %bitcast.55), channel_id=1, source_target_pairs={{1,0},{2,1},{3,2},{4,3},{5,4},{6,5},{7,6},{8,7},{9,8},{10,9},{11,1... | collective-permute-start | bytes 3145736 | tf_op jit(solution)/shard_map/ppermute | solution.py:19
  505.5 22.4 %collective-permute-start.3 = (f32[8,1,128,256]{3,0,2,1:T(8,128)S(1)}, f32[8,1,128,256]{3,0,2,1:T(8,128)S(1)}, u32[]{:S(2)}, u32[]{:S(2)}) collective-permute-start(f32[8,1,128,256]{3,0,2,1:T(8,128)S(1)} %bitcast.56), channel_id=1, source_target_pairs={{0,1},{1,2},{2,3},{3,4},{4,5},{5,6},{6,7},{7,8},{8,9},{9,10},{10,1... | collective-permute-start | bytes 3145736 | tf_op jit(solution)/shard_map/ppermute | solution.py:16
  527.9 1.7 copy-start.1
  528.6 1.0 copy-start.9
  662.4 29.5 %copy-start.3 = (f32[8,32768]{1,0:T(8,128)}, f32[8,32768]{1,0:T(8,128)S(1)}, u32[]{:S(2)}) copy-start(f32[8,32768]{1,0:T(8,128)S(1)} %fusion.1) | copy-start | bytes 3145732
  662.4 28.9 %collective-permute-start.4 = (f32[8,1,128,256]{3,0,2,1:T(8,128)S(1)}, f32[8,1,128,256]{3,0,2,1:T(8,128)S(1)}, u32[]{:S(2)}, u32[]{:S(2)}) collective-permute-start(f32[8,1,128,256]{3,0,2,1:T(8,128)S(1)} %bitcast.50), channel_id=1, source_target_pairs={{1,0},{2,1},{3,2},{4,3},{5,4},{6,5},{7,6},{8,7},{9,8},{10,9},{11,1... | collective-permute-start | bytes 3145736 | tf_op jit(solution)/shard_map/ppermute | solution.py:19
  666.6 24.7 %collective-permute-start.5 = (f32[8,1,128,256]{3,0,2,1:T(8,128)S(1)}, f32[8,1,128,256]{3,0,2,1:T(8,128)S(1)}, u32[]{:S(2)}, u32[]{:S(2)}) collective-permute-start(f32[8,1,128,256]{3,0,2,1:T(8,128)S(1)} %bitcast.51), channel_id=1, source_target_pairs={{0,1},{1,2},{2,3},{3,4},{4,5},{5,6},{6,7},{7,8},{8,9},{9,10},{10,1... | collective-permute-start | bytes 3145736 | tf_op jit(solution)/shard_map/ppermute | solution.py:16
  691.3 1.7 copy-start.2
  691.9 1.0 copy-start.7
  824.7 1.6 copy-start.10
Sparse Core Ops, SparseCore 0:
  10.0 48.8 all-gather.2
  827.8 42.2 reduce-scatter.1
where the time goes:
time: 988 us; the launch traced here: 987 us
  blocking collectives  749 us (76%)
  waiting for transfers between devices  149 us (15%)
  matrix products  31.7 us (3%)
  starting transfers between devices  22.8 us (2%)
  local copies, waits for them, and re-layouts  14.8 us (1%)
  between operations  14.4 us (1%)
    psum x5, blocking collectives, project_slab(): intersection = lax.psum(intersection, 'xy') / cell_total  640 us
    psum x1, blocking collectives, local(): response_matrix = lax.psum(local_sum, ('band', 'xy')) / cell_total  109 us
    ppermute x3, waiting for transfers between devices, padded_2(): lax.ppermute(lax.slice_in_dim(block, 0, width, axis=dim), axis, backward)  62.5 us
    all_gather x1, waiting for transfers between devices, local(): psi_all = lax.all_gather(psi_flat, 'band', axis=0, tiled=True)  45.2 us
    reduce_scatter x1, waiting for transfers between devices, local(): lax.psum_scatter(partial_grid, 'band', scatter_dimension=2, tiled=True)  41.6 us
  transfers between devices with their start and end apart: 8, of which 5 were waited for; matrix products, arithmetic and copies ran while one was open for 1% of the time, Pallas kernels for 0%

commit v1 on v0

--- a/solution.py
+++ b/solution.py
@@ -93,7 +93,12 @@
         precision=highest,
         preferred_element_type=jnp.float32,
     )
-    response_matrix = lax.psum(local_sum, ("band", "xy")) / cell_total
+
+    def cover_scenes(w_in):
+        vec_out = jnp.sum(lax.all_gather(w_in, axis_name=("band", "xy")), axis=0)
+        return vec_out
+
+    response_matrix = cover_scenes(local_sum) / cell_total
     return (density, response_matrix)
 
 

time: 988 us -> 1570 us (1.59)
  blocking collectives: 749 us -> 1330 us
    all_gather x0 -> x1, blocking collectives: none -> 690 us  [cover_scenes(): vec_out = jnp.sum(lax.all_gather(w_in, axis_name=('band', 'xy')), axis=0)]
    psum x1 -> x0, blocking collectives: 109 us -> none  [local(): response_matrix = lax.psum(local_sum, ('band', 'xy')) / cell_total]
  transfers between devices with their start and end apart: 8 -> 8, of which waited for: 5 -> 5; matrix products, arithmetic and copies ran while one was open for 1% -> 0% of each run, Pallas kernels for 0% -> 0%
where the time goes in v1:
time: 1570 us
  blocking collectives  1330 us (85%)
  waiting for transfers between devices  149 us (9%)
  matrix products  31.7 us (2%)
  starting transfers between devices  22.8 us (1%)
    all_gather x1, blocking collectives, cover_scenes(): vec_out = jnp.sum(lax.all_gather(w_in, axis_name=('band', 'xy')), axis=0)  690 us
    psum x5, blocking collectives, project_slab(): intersection = lax.psum(intersection, 'xy') / cell_total  640 us
    ppermute x3, waiting for transfers between devices, padded_2(): lax.ppermute(lax.slice_in_dim(block, 0, width, axis=dim), axis, backward)  62.5 us
    all_gather x1, waiting for transfers between devices, local(): psi_all = lax.all_gather(psi_flat, 'band', axis=0, tiled=True)  45.2 us
    reduce_scatter x1, waiting for transfers between devices, local(): lax.psum_scatter(partial_grid, 'band', scatter_dimension=2, tiled=True)  41.6 us
  transfers between devices with their start and end apart: 8, of which 5 were waited for; matrix products, arithmetic and copies ran while one was open for 0% of the time, Pallas kernels for 0%

profile of v1, /device:TPU:1, one launch (start us, length us, event | category | flops | bytes accessed | tf_op | source)
XLA Modules:
  0.0 1569.2 jit_solution(9935744630120468647)
XLA Ops:
  7.2 1.8 reshape.122
  12.4 1.4 mul.77
  13.7 45.2 %all-gather.5.cloned.1.call-done = f32[8,2,32768]{2,1,0:T(2,128)} async-done(((f32[1,2,32768]{2,1,0:T(2,128)}), f32[8,2,32768]{2,1,0:T(2,128)}) %all-gather.5.cloned.1.call-update) | async-done | bytes 2097168 | tf_op jit(solution)/shard_map/all_gather | solution.py:58
  58.9 2.7 reshape.123
  61.6 3.8 convolution_bitcast_fusion.4
  65.4 135.0 %psum.35 = f32[16,8]{0,1:T(8,128)S(1)} all-reduce(f32[16,8]{0,1:T(8,128)S(1)} %convolution_bitcast_fusion.4), channel_id=1, replica_groups=mesh['band'=8,'xy'=64] {'xy'}, use_global_device_ids=true, to_apply=%region_0.0 | all-reduce | flops 128 | bytes 1024 | tf_op jit(solution)/shard_map/psum | solution.py:64
  200.4 3.4 fusion.40
  204.8 2.5 convolution_bitcast_fusion.3
  207.4 128.3 %psum.36 = f32[16,8]{0,1:T(8,128)S(1)} all-reduce(f32[16,8]{0,1:T(8,128)S(1)} %convolution_bitcast_fusion.3), channel_id=1, replica_groups=mesh['band'=8,'xy'=64] {'xy'}, use_global_device_ids=true, to_apply=%region_1.0 | all-reduce | flops 128 | bytes 1024 | tf_op jit(solution)/shard_map/psum | solution.py:64
  335.7 2.3 convolution_subtract_fusion.3
  338.0 2.9 collective-permute-start
  340.9 4.4 collective-permute-start.1
  345.4 21.4 %collective-permute-done = f32[8,1,128,256]{3,0,2,1:T(8,128)S(1)} collective-permute-done((f32[8,1,128,256]{3,0,2,1:T(8,128)S(1)}, f32[8,1,128,256]{3,0,2,1:T(8,128)S(1)}, u32[]{:S(2)}, u32[]{:S(2)}) %collective-permute-start) | collective-permute-done | bytes 1048608 | tf_op jit(solution)/shard_map/ppermute | solution.py:19
  368.5 2.7 convolution_bitcast_fusion.2
  371.2 124.7 %psum.37 = f32[16,8]{0,1:T(8,128)S(1)} all-reduce(f32[16,8]{0,1:T(8,128)S(1)} %convolution_bitcast_fusion.2), channel_id=1, replica_groups=mesh['band'=8,'xy'=64] {'xy'}, use_global_device_ids=true, to_apply=%region_2.3 | all-reduce | flops 128 | bytes 1024 | tf_op jit(solution)/shard_map/psum | solution.py:64
  495.9 3.1 fusion.2
  499.1 6.5 collective-permute-start.2
  505.5 1.9 collective-permute-start.3
  507.7 20.3 %collective-permute-done.2 = f32[8,1,128,256]{3,0,2,1:T(8,128)S(1)} collective-permute-done((f32[8,1,128,256]{3,0,2,1:T(8,128)S(1)}, f32[8,1,128,256]{3,0,2,1:T(8,128)S(1)}, u32[]{:S(2)}, u32[]{:S(2)}) %collective-permute-start.2) | collective-permute-done | bytes 1048608 | tf_op jit(solution)/shard_map/ppermute | solution.py:19
  529.6 2.7 convolution_bitcast_fusion.1
  532.3 127.0 %psum.38 = f32[16,8]{0,1:T(8,128)S(1)} all-reduce(f32[16,8]{0,1:T(8,128)S(1)} %convolution_bitcast_fusion.1), channel_id=1, replica_groups=mesh['band'=8,'xy'=64] {'xy'}, use_global_device_ids=true, to_apply=%region_3.4 | all-reduce | flops 128 | bytes 1024 | tf_op jit(solution)/shard_map/psum | solution.py:64
  659.3 3.1 fusion.1
  662.4 4.2 collective-permute-start.4
  666.6 2.9 collective-permute-start.5
  670.5 20.8 %collective-permute-done.4 = f32[8,1,128,256]{3,0,2,1:T(8,128)S(1)} collective-permute-done((f32[8,1,128,256]{3,0,2,1:T(8,128)S(1)}, f32[8,1,128,256]{3,0,2,1:T(8,128)S(1)}, u32[]{:S(2)}, u32[]{:S(2)}) %collective-permute-start.4) | collective-permute-done | bytes 1048608 | tf_op jit(solution)/shard_map/ppermute | solution.py:19
  692.9 2.7 convolution_bitcast_fusion
  695.6 124.9 %psum.39 = f32[16,8]{0,1:T(8,128)S(1)} all-reduce(f32[16,8]{0,1:T(8,128)S(1)} %convolution_bitcast_fusion), channel_id=1, replica_groups=mesh['band'=8,'xy'=64] {'xy'}, use_global_device_ids=true, to_apply=%region_4.5 | all-reduce | flops 128 | bytes 1024 | tf_op jit(solution)/shard_map/psum | solution.py:64
  820.5 4.1 fusion
  824.7 1.6 reshape.118
  828.6 41.6 %reduce-scatter.2.cloned.1.call-done = f32[4,1,16,256]{3,2,1,0:T(8,128)} async-done(((f32[4,1,128,256]{3,2,1,0:T(8,128)}), f32[4,1,16,256]{3,2,1,0:T(8,128)}) %reduce-scatter.2.cloned.1.call-update) | async-done | bytes 65552 | tf_op jit(solution)/shard_map/reduce_scatter | solution.py:89
  870.1 1.2 convolution_bitcast_fusion.5
  871.4 689.9 %all-gather.2 = f32[512,4,4]{2,1,0:T(4,128)S(1)} all-gather(f32[1,4,4]{2,1,0:T(4,128)S(1)} %convolution_bitcast_fusion.5), channel_id=2, replica_groups=mesh['band'=8,'xy'=64] {'band','xy'}, dimensions={0}, use_global_device_ids=true | all-gather | bytes 32832 | tf_op jit(solution)/shard_map/all_gather | solution.py:98
  (60 shorter events, 13.9 us)
Async XLA Ops:
  7.2 51.8 %all-gather.5.cloned.1.call-start = ((), (), s32[]{:S(2)}) async-start(), calls=%async_computation.2 | async-start | bytes 2359296 | tf_op jit(solution)/shard_map/all_gather | solution.py:58
  9.1 861.1 %reduce-scatter.2.cloned.1.call-start = ((), (), s32[]{:S(2)}) async-start(), calls=%async_computation.1 | async-start | bytes 589824 | tf_op jit(solution)/shard_map/reduce_scatter | solution.py:89
  10.0 1.5 copy-start.11
  10.1 1.7 copy-start.12
  203.9 1.0 copy-start.6
  338.0 29.5 %copy-start.5 = (f32[8,32768]{1,0:T(8,128)}, f32[8,32768]{1,0:T(8,128)S(1)}, u32[]{:S(2)}) copy-start(f32[8,32768]{1,0:T(8,128)S(1)} %convolution_subtract_fusion.3) | copy-start | bytes 3145732
  338.0 28.9 %collective-permute-start = (f32[8,1,128,256]{3,0,2,1:T(8,128)S(1)}, f32[8,1,128,256]{3,0,2,1:T(8,128)S(1)}, u32[]{:S(2)}, u32[]{:S(2)}) collective-permute-start(f32[8,1,128,256]{3,0,2,1:T(8,128)S(1)} %bitcast.61), channel_id=1, source_target_pairs={{1,0},{2,1},{3,2},{4,3},{5,4},{6,5},{7,6},{8,7},{9,8},{10,9},{11,1... | collective-permute-start | bytes 3145736 | tf_op jit(solution)/shard_map/ppermute | solution.py:19
  340.9 26.0 %collective-permute-start.1 = (f32[8,1,128,256]{3,0,2,1:T(8,128)S(1)}, f32[8,1,128,256]{3,0,2,1:T(8,128)S(1)}, u32[]{:S(2)}, u32[]{:S(2)}) collective-permute-start(f32[8,1,128,256]{3,0,2,1:T(8,128)S(1)} %bitcast.62), channel_id=1, source_target_pairs={{0,1},{1,2},{2,3},{3,4},{4,5},{5,6},{6,7},{7,8},{8,9},{9,10},{10,1... | collective-permute-start | bytes 3145736 | tf_op jit(solution)/shard_map/ppermute | solution.py:16
  366.9 1.7 copy-start
  367.5 1.0 copy-start.8
  495.9 11.6 copy-start.13
  499.1 29.5 %copy-start.4 = (f32[8,32768]{1,0:T(8,128)}, f32[8,32768]{1,0:T(8,128)S(1)}, u32[]{:S(2)}) copy-start(f32[8,32768]{1,0:T(8,128)S(1)} %fusion.2) | copy-start | bytes 3145732
  499.1 28.9 %collective-permute-start.2 = (f32[8,1,128,256]{3,0,2,1:T(8,128)S(1)}, f32[8,1,128,256]{3,0,2,1:T(8,128)S(1)}, u32[]{:S(2)}, u32[]{:S(2)}) collective-permute-start(f32[8,1,128,256]{3,0,2,1:T(8,128)S(1)} %bitcast.56), channel_id=1, source_target_pairs={{1,0},{2,1},{3,2},{4,3},{5,4},{6,5},{7,6},{8,7},{9,8},{10,9},{11,1... | collective-permute-start | bytes 3145736 | tf_op jit(solution)/shard_map/ppermute | solution.py:19
  505.5 22.4 %collective-permute-start.3 = (f32[8,1,128,256]{3,0,2,1:T(8,128)S(1)}, f32[8,1,128,256]{3,0,2,1:T(8,128)S(1)}, u32[]{:S(2)}, u32[]{:S(2)}) collective-permute-start(f32[8,1,128,256]{3,0,2,1:T(8,128)S(1)} %bitcast.57), channel_id=1, source_target_pairs={{0,1},{1,2},{2,3},{3,4},{4,5},{5,6},{6,7},{7,8},{8,9},{9,10},{10,1... | collective-permute-start | bytes 3145736 | tf_op jit(solution)/shard_map/ppermute | solution.py:16
  527.9 1.7 copy-start.1
  528.6 1.0 copy-start.9
  662.4 29.5 %copy-start.3 = (f32[8,32768]{1,0:T(8,128)}, f32[8,32768]{1,0:T(8,128)S(1)}, u32[]{:S(2)}) copy-start(f32[8,32768]{1,0:T(8,128)S(1)} %fusion.1) | copy-start | bytes 3145732
  662.4 28.9 %collective-permute-start.4 = (f32[8,1,128,256]{3,0,2,1:T(8,128)S(1)}, f32[8,1,128,256]{3,0,2,1:T(8,128)S(1)}, u32[]{:S(2)}, u32[]{:S(2)}) collective-permute-start(f32[8,1,128,256]{3,0,2,1:T(8,128)S(1)} %bitcast.51), channel_id=1, source_target_pairs={{1,0},{2,1},{3,2},{4,3},{5,4},{6,5},{7,6},{8,7},{9,8},{10,9},{11,1... | collective-permute-start | bytes 3145736 | tf_op jit(solution)/shard_map/ppermute | solution.py:19
  666.6 24.7 %collective-permute-start.5 = (f32[8,1,128,256]{3,0,2,1:T(8,128)S(1)}, f32[8,1,128,256]{3,0,2,1:T(8,128)S(1)}, u32[]{:S(2)}, u32[]{:S(2)}) collective-permute-start(f32[8,1,128,256]{3,0,2,1:T(8,128)S(1)} %bitcast.52), channel_id=1, source_target_pairs={{0,1},{1,2},{2,3},{3,4},{4,5},{5,6},{6,7},{7,8},{8,9},{9,10},{10,1... | collective-permute-start | bytes 3145736 | tf_op jit(solution)/shard_map/ppermute | solution.py:16
  691.3 1.7 copy-start.2
  691.9 1.0 copy-start.7
  824.7 1.6 copy-start.10
Sparse Core Ops, SparseCore 0:
  10.0 48.8 all-gather.4
  827.8 42.2 reduce-scatter.1
